TPU v7x, 256 devices: a whole 4x4x8 slice. The times are simulated.
256 devices in a mesh: ctx: 32 (over x, z), head: 8 (over y, core).
Axes of the slice: x: 4, y: 4, z: 8, core: 2. Of those that a mesh axis runs over, the one named last changes fastest.
Arguments:
- features: bfloat16 [8192, 16384], P('ctx', 'head'), may hold values from -6 to 6
- log_decay: float32 [256, 8192], P('head', 'ctx'), may hold values from -2 to 0, as said below
- step_size: float32 [256, 8192], P('head', 'ctx'), may hold values from 0.0002 to 0.002
- b_matrix: bfloat16 [8192, 2048], P('ctx', 'head'), may hold values from -6 to 6
- c_matrix: bfloat16 [8192, 2048], P('ctx', 'head'), may hold values from -6 to 6
- skip_gain: float32 [256], P('head'), may hold values from 0.5 to 1.5
Outputs:
- mixed: bfloat16 [8192, 16384], P('ctx', 'head')
Inputs may be any that keep to these rules, and one draw needn't show every extreme that they name: `log_decay`: every entry is negative.
All inputs are finite; a program needn't handle non-finite values.
Results may differ from a plain program's by a relative error of at most 0.0013.
Values sent between devices are 32-bit elements; how exact they have to be, the bound alone decides.
No kernel may reach another device: no remote copies, remote signals or barrier semaphores. Data moves between devices by JAX's collectives and lax.ppermute only.
A program may use at most 320 MiB of HBM per device.

v0:
```python
import jax
import jax.numpy as jnp
import numpy as np
from jax import lax
from jax.sharding import PartitionSpec as P

N = 256
SPAN = 128


def chain_mixing(decay, devices, halves):
    j = np.arange(devices)
    pos = np.stack([j, halves * devices - 1 - j], axis=1).reshape(-1)
    between = (pos[None, :, None] < pos[None, None, :]) & (pos[None, None, :] < pos[:, None, None])
    gap = jnp.sum(jnp.where(between[None], decay[:, None, None, :], 0.0), axis=-1)
    lower = pos[None, :] < pos[:, None]
    mixing = jnp.where(lower[None], jnp.exp(gap), 0.0)
    return mixing.reshape(-1, devices, halves, devices, halves)


def on_device(features, log_decay, step_size, b_matrix, c_matrix, skip_gain):
    head_count = log_decay.shape[0]
    tok_rows = features.shape[0]
    head_width = features.shape[1] // head_count
    state_size = N
    group_count = b_matrix.shape[1] // state_size
    per_group = head_count // group_count
    halves = tok_rows // SPAN
    assert halves == 2
    devices = lax.axis_size("ctx")
    per_chunk = head_count // devices
    flat = head_width * state_size
    rows = halves * head_width
    extra = 8
    cumulative = jnp.cumsum(log_decay.reshape(head_count, halves, SPAN), axis=2)
    totals = cumulative[:, :, -1]
    step_rows = step_size.reshape(head_count, halves, SPAN)
    grouped_inputs = features.reshape(halves, SPAN, group_count, per_group, head_width)
    b_spans = b_matrix.reshape(halves, SPAN, group_count, state_size)
    c_spans = c_matrix.reshape(halves, SPAN, group_count, state_size)
    coeffs = jnp.exp(totals[:, :, None] - cumulative) * step_rows
    coeffs = jnp.transpose(coeffs.reshape(group_count, per_group, halves, SPAN), (2, 3, 0, 1))
    weighted = (grouped_inputs * coeffs[..., None]).astype(jnp.bfloat16)
    span_states = jnp.einsum(
        "ksgn,ksgqp->gqkpn", b_spans, weighted, preferred_element_type=jnp.float32
    ).reshape(head_count, rows, state_size)
    me = lax.axis_index("ctx")
    spread = jnp.zeros((devices, halves, head_count), jnp.float32)
    spread = lax.dynamic_update_slice_in_dim(spread, jnp.transpose(totals)[None], me, axis=0)
    all_decay = lax.psum(spread, "ctx")
    got = lax.all_to_all(span_states, "ctx", 0, 0, tiled=True)
    got_states = got.reshape(devices, per_chunk, halves, head_width, state_size)
    mine = lax.dynamic_slice_in_dim(all_decay, me * per_chunk, per_chunk, axis=2)
    mixing = chain_mixing(
        jnp.transpose(mine, (2, 0, 1)).reshape(per_chunk, devices * halves), devices, halves
    )
    j = np.arange(devices)
    own = np.zeros((devices, halves, devices, halves), bool)
    own[j, 1, j, 0] = True
    others = jnp.where(own[None], 0.0, mixing)
    if per_chunk == 1:
        solved = jnp.einsum(
            "uv,vpn->upn",
            others.reshape(devices * halves, devices * halves),
            got.reshape(devices * halves, head_width, state_size),
            precision=lax.Precision.HIGHEST,
            preferred_element_type=jnp.float32,
        ).reshape(devices, rows, state_size)
    else:
        solved = jnp.einsum(
            "cjkJL,JcLpn->jckpn",
            others,
            got_states,
            precision=lax.Precision.HIGHEST,
            preferred_element_type=jnp.float32,
        ).reshape(devices * per_chunk, rows, state_size)
    back = lax.all_to_all(solved, "ctx", 0, 0, tiled=True)
    later = np.arange(devices)[:, None] > me
    gain = jnp.exp(jnp.sum(jnp.where(later, jnp.sum(all_decay, axis=1), 0.0), axis=0))
    state_halves = [
        back[:, :head_width].astype(jnp.bfloat16).reshape(head_count * head_width, state_size),
        (back[:, head_width:rows] + gain[:, None, None] * span_states[:, :head_width])
        .astype(jnp.bfloat16)
        .reshape(head_count * head_width, state_size),
    ]
    scores = jnp.einsum("ktgn,ksgn->gkts", c_spans, b_spans, preferred_element_type=jnp.float32)
    causal = jnp.arange(SPAN)[:, None] >= jnp.arange(SPAN)[None, :]
    cum_grouped = cumulative.reshape(group_count, per_group, halves, SPAN)
    step_grouped = step_rows.reshape(group_count, per_group, halves, SPAN)
    decay_gaps = jnp.where(causal, cum_grouped[..., :, None] - cum_grouped[..., None, :], -jnp.inf)
    weights = (scores[:, None] * jnp.exp(decay_gaps) * step_grouped[:, :, :, None, :]).astype(
        jnp.bfloat16
    )
    diagonal_part = jnp.einsum(
        "gqkts,ksgqp->ktgqp", weights, grouped_inputs, preferred_element_type=jnp.float32
    ).reshape(halves, SPAN, head_count * head_width)
    decay_in = jnp.repeat(jnp.transpose(jnp.exp(cumulative), (1, 2, 0)), head_width, axis=2)
    skip = jnp.repeat(skip_gain, head_width)[None, :]
    inputs = features.reshape(halves, SPAN, head_count * head_width).astype(jnp.float32)
    per_group_width = per_group * head_width
    outs = []
    for k in range(halves):
        state_part = jnp.concatenate(
            [
                jnp.dot(
                    c_spans[k, :, g],
                    state_halves[k][g * per_group_width : (g + 1) * per_group_width].T,
                    preferred_element_type=jnp.float32,
                )
                for g in range(group_count)
            ],
            axis=1,
        )
        outs.append(diagonal_part[k] + state_part * decay_in[k] + skip * inputs[k])
    return jnp.concatenate(outs, axis=0).astype(jnp.bfloat16)


def solution(mesh):
    placed = (
        P("ctx", "head"),
        P("head", "ctx"),
        P("head", "ctx"),
        P("ctx", "head"),
        P("ctx", "head"),
        P("head"),
    )
    return jax.shard_map(
        on_device, mesh=mesh, in_specs=placed, out_specs=P("ctx", "head"), check_vma=False
    )
```

profile of v0, /device:TPU:16, one launch (start us, length us, event | category | flops | bytes accessed | tf_op | source)
XLA Modules:
  0.0 344.3 jit_solution(12947823522675433255)
XLA Ops:
  0.0 0.8 copy_bitcast_fusion.1
  0.8 0.6 reduce_window_sum.13
  1.5 0.8 reshape.145
  2.4 1.5 copy.52
  4.2 1.1 multiply_convert_fusion.2
  5.3 0.7 convolution_bitcast_fusion.2
  6.0 2.2 copy.58
  8.3 11.6 %all-to-all-start = ((f32[32,128,256]{2,1,0:T(8,128)}), f32[32,128,256]{2,1,0:T(8,128)}, u32[]{:S(2)}, u32[]{:S(2)}) async-start(f32[32,128,256]{2,1,0:T(8,128)} %bitcast.92), calls=%async_computation | async-start | bytes 8388608 | tf_op jit(solution)/shard_map/all_to_all | solution.py:51
  20.1 232.9 %psum.7 = f32[32,2,32]{1,0,2:T(8,128)S(1)} all-reduce(f32[32,2,32]{1,0,2:T(8,128)S(1)} %dynamic_update_slice.3), channel_id=1, replica_groups=mesh['ctx'=32,'head'=8] {'ctx'}, use_global_device_ids=true, to_apply=%region_1.2 | all-reduce | flops 2048 | bytes 16384 | tf_op jit(solution)/shard_map/psum | solution.py:50
  253.1 0.6 select_reduce_fusion
  253.8 8.4 %fusion = f32[64,64,256]{2,0,1:T(8,128)S(1)} fusion(f32[64,64,256]{2,1,0:T(8,128)} %bitcast.17, pred[64,64]{1,0:T(32,128)(4,1)S(1)} %copy-done.11, pred[64,64]{1,0:T(32,128)(4,1)S(1)} %copy-done.10, f32[64,64]{1,0:T(8,128)S(1)} %select_reduce_fusion), kind=kOutput, calls=%fused_computation | convolution fusion | flops 805314560 | bytes 8413184 | tf_op jit(solution)/shard_map/uv,vpn->upn/dot_general | solution.py:62
  262.2 4.4 %copy.60 = f32[64,64,256]{2,1,0:T(8,128)} copy(f32[64,64,256]{2,0,1:T(8,128)S(1)} %fusion) | data formatting | bytes 8388608 | tf_op jit(solution)/shard_map/uv,vpn->upn/dot_general | solution.py:62
  266.6 5.2 %all-to-all-start.1 = ((f32[32,128,256]{2,1,0:T(8,128)}), f32[32,128,256]{2,1,0:T(8,128)}, u32[]{:S(2)}, u32[]{:S(2)}) async-start(f32[32,128,256]{2,1,0:T(8,128)} %bitcast.94), calls=%async_computation.1 | async-start | bytes 8388608 | tf_op jit(solution)/shard_map/all_to_all | solution.py:77
  272.6 3.6 %fusion.19 = f32[2,128,1,32,64]{1,4,3,0,2:T(8,128)S(1)} fusion(f32[32,2,128]{2,0,1:T(8,128)S(1)} %copy_bitcast_fusion, f32[32,2,128]{2,0,1:T(8,128)S(1)} %reduce_window_sum.13, f32[2,128,128]{2,1,0:T(8,128)S(1)} %fusion.35, pred[128,128]{1,0:T(8,128)(4,1)S(1)} %iota_compare_fusion, bf16[2,128,32,64]{1,0,3,2:T(2,128)(2,1)} %copy-done.2), kind=kOutput, calls=%fused_computation.27 | convolution fusion | flops 139460608 | bytes 3358720 | tf_op jit(solution)/shard_map/gqkts,ksgqp->ktgqp/dot_general | solution.py:94
  276.2 1.2 fusion.34
  277.4 1.3 copy.64
  278.8 1.3 copy.63
  280.3 2.6 copy.62
  283.0 1.3 copy.61
  284.3 53.5 %all-to-all-done.1 = f32[32,128,256]{2,1,0:T(8,128)} async-done(((f32[32,128,256]{2,1,0:T(8,128)}), f32[32,128,256]{2,1,0:T(8,128)}, u32[]{:S(2)}, u32[]{:S(2)}) %all-to-all-start.1) | async-done | bytes 4194336 | tf_op jit(solution)/shard_map/all_to_all | solution.py:77
  337.8 2.6 fusion.12
  340.4 0.5 fusion.8
  340.9 1.8 slice.95
  343.3 1.1 pad_maximum_fusion
  (53 shorter events, 2.5 us)
Async XLA Ops:
  0.0 5.3 %copy-start = (bf16[256,256]{1,0:T(8,128)(2,1)S(1)}, bf16[256,256]{1,0:T(8,128)(2,1)}, u32[]{:S(2)}) copy-start(bf16[256,256]{1,0:T(8,128)(2,1)} %param.13) | copy-start | bytes 393220
  4.2 4.0 %copy-start.2 = (bf16[2,128,32,64]{1,0,3,2:T(2,128)(2,1)}, bf16[2,128,32,64]{1,0,3,2:T(2,128)(2,1)S(1)}, u32[]{:S(2)}) copy-start(bf16[2,128,32,64]{1,0,3,2:T(2,128)(2,1)S(1)} %reshape.142) | copy-start | bytes 3145732
  8.3 244.9 %copy-start.8 = (pred[1,64,64,64]{3,2,1,0:T(32,128)(4,1)S(1)}, pred[1,64,64,64]{3,2,1,0:T(32,128)(4,1)}, u32[]{:S(2)}) copy-start(pred[1,64,64,64]{3,2,1,0:T(32,128)(4,1)} %constant.26.clone) | copy-start | bytes 786436
  8.3 245.5 %copy-start.10 = (pred[64,64]{1,0:T(32,128)(4,1)S(1)}, pred[64,64]{1,0:T(32,128)(4,1)}, u32[]{:S(2)}) copy-start(pred[64,64]{1,0:T(32,128)(4,1)} %constant.31) | copy-start | bytes 12292
  8.3 245.5 %copy-start.11 = (pred[64,64]{1,0:T(32,128)(4,1)S(1)}, pred[64,64]{1,0:T(32,128)(4,1)}, u32[]{:S(2)}) copy-start(pred[64,64]{1,0:T(32,128)(4,1)} %constant.32) | copy-start | bytes 12292
  8.3 245.5 %all-to-all-start = ((f32[32,128,256]{2,1,0:T(8,128)}), f32[32,128,256]{2,1,0:T(8,128)}, u32[]{:S(2)}, u32[]{:S(2)}) async-start(f32[32,128,256]{2,1,0:T(8,128)} %bitcast.92), calls=%async_computation | async-start | bytes 8388608 | tf_op jit(solution)/shard_map/all_to_all | solution.py:51
  266.6 5.4 %copy-start.1 = (bf16[256,2048]{1,0:T(8,128)(2,1)S(1)}, bf16[256,2048]{1,0:T(8,128)(2,1)}, u32[]{:S(2)}) copy-start(bf16[256,2048]{1,0:T(8,128)(2,1)} %param.10) | copy-start | bytes 3145732
  266.6 5.7 %copy-start.13 = (s32[32,1]{0,1:T(1,128)S(1)}, s32[32,1]{0,1:T(1,128)}, u32[]{:S(2)}) copy-start(s32[32,1]{0,1:T(1,128)} %constant.29.clone) | copy-start | bytes 388
  266.6 5.8 %copy-start.9 = (f32[32,256]{1,0:T(8,128)S(1)}, f32[32,256]{1,0:T(8,128)}, u32[]{:S(2)}) copy-start(f32[32,256]{1,0:T(8,128)} %param.12) | copy-start | bytes 98308
  266.6 5.9 %copy-start.7 = (bf16[256,256]{1,0:T(8,128)(2,1)S(1)}, bf16[256,256]{1,0:T(8,128)(2,1)}, u32[]{:S(2)}) copy-start(bf16[256,256]{1,0:T(8,128)(2,1)} %param.14) | copy-start | bytes 393220
  266.6 71.2 %all-to-all-start.1 = ((f32[32,128,256]{2,1,0:T(8,128)}), f32[32,128,256]{2,1,0:T(8,128)}, u32[]{:S(2)}, u32[]{:S(2)}) async-start(f32[32,128,256]{2,1,0:T(8,128)} %bitcast.94), calls=%async_computation.1 | async-start | bytes 8388608 | tf_op jit(solution)/shard_map/all_to_all | solution.py:77
  276.2 3.9 %copy-start.12 = (f32[32]{0:T(128)S(1)}, f32[32]{0:T(128)}, u32[]{:S(2)}) copy-start(f32[32]{0:T(128)} %param.15) | copy-start | bytes 388
  284.3 56.1 %copy-start.3 = (f32[128,2048]{1,0:T(8,128)S(1)}, f32[128,2048]{1,0:T(8,128)}, u32[]{:S(2)}) copy-start(f32[128,2048]{1,0:T(8,128)} %copy.64) | copy-start | bytes 3145732
  337.8 2.6 copy-start.5
  340.4 2.4 copy-start.4
  340.4 2.4 copy-start.6
where the time goes:
time: 345 us; the launch traced here: 344 us
  blocking collectives  233 us (68%)
  waiting for transfers between devices  53.5 us (16%)
  local copies, waits for them, and re-layouts  20.4 us (6%)
  starting transfers between devices  16.8 us (5%)
  matrix products  13.9 us (4%)
  other arithmetic  6.54 us (2%)
    psum x1, blocking collectives, on_device(): all_decay = lax.psum(spread, 'ctx')  233 us
    all_to_all x1, waiting for transfers between devices, on_device(): back = lax.all_to_all(solved, 'ctx', 0, 0, tiled=True)  53.5 us
    all_to_all x1, starting transfers between devices, on_device(): got = lax.all_to_all(span_states, 'ctx', 0, 0, tiled=True)  11.6 us
    dot_general x1, matrix products, on_device(): jnp.einsum('uv,vpn->upn', others.reshape(devices * halves, devices * halv...  8.4 us
  transfers between devices with their start and end apart: 2, of which 1 were waited for; matrix products, arithmetic and copies ran while one was open for 4% of the time, Pallas kernels for 0%

commit v1 on v0

--- a/solution.py
+++ b/solution.py
@@ -47,7 +47,7 @@
     me = lax.axis_index("ctx")
     spread = jnp.zeros((devices, halves, head_count), jnp.float32)
     spread = lax.dynamic_update_slice_in_dim(spread, jnp.transpose(totals)[None], me, axis=0)
-    all_decay = lax.psum(spread, "ctx")
+    all_decay = jnp.sum(lax.all_gather(spread, "ctx"), axis=0)
     got = lax.all_to_all(span_states, "ctx", 0, 0, tiled=True)
     got_states = got.reshape(devices, per_chunk, halves, head_width, state_size)
     mine = lax.dynamic_slice_in_dim(all_decay, me * per_chunk, per_chunk, axis=2)

time: 345 us -> 271 us (0.79)
  blocking collectives: 233 us -> 137 us
  waiting for transfers between devices: 53.5 us -> 73.6 us
    psum x1 -> x0, blocking collectives: 233 us -> none  [on_device(): all_decay = lax.psum(spread, 'ctx')]
    all_gather x0 -> x1, blocking collectives: none -> 137 us  [on_device(): all_decay = jnp.sum(lax.all_gather(spread, 'ctx'), axis=0)]
    all_to_all x1, waiting for transfers between devices: 53.5 us -> 73.6 us  [on_device(): back = lax.all_to_all(solved, 'ctx', 0, 0, tiled=True)]
  transfers between devices with their start and end apart: 2 -> 2, of which waited for: 1 -> 1; matrix products, arithmetic and copies ran while one was open for 4% -> 5% of each run, Pallas kernels for 0% -> 0%
where the time goes in v1:
time: 271 us
  blocking collectives  137 us (51%)
  waiting for transfers between devices  73.6 us (27%)
  local copies, waits for them, and re-layouts  20.4 us (8%)
  starting transfers between devices  19.3 us (7%)
  matrix products  13.9 us (5%)
  other arithmetic  6.44 us (2%)
    all_gather x1, blocking collectives, on_device(): all_decay = jnp.sum(lax.all_gather(spread, 'ctx'), axis=0)  137 us
    all_to_all x1, waiting for transfers between devices, on_device(): back = lax.all_to_all(solved, 'ctx', 0, 0, tiled=True)  73.6 us
    all_to_all x1, starting transfers between devices, on_device(): got = lax.all_to_all(span_states, 'ctx', 0, 0, tiled=True)  11.6 us
    dot_general x1, matrix products, on_device(): jnp.einsum('uv,vpn->upn', others.reshape(devices * halves, devices * halv...  8.4 us
    all_to_all x1, starting transfers between devices, on_device(): back = lax.all_to_all(solved, 'ctx', 0, 0, tiled=True)  7.7 us
  transfers between devices with their start and end apart: 2, of which 1 were waited for; matrix products, arithmetic and copies ran while one was open for 5% of the time, Pallas kernels for 0%

profile of v1, /device:TPU:16, one launch (start us, length us, event | category | flops | bytes accessed | tf_op | source)
XLA Modules:
  0.0 270.6 jit_solution(3616762329713386177)
XLA Ops:
  0.0 0.8 copy_bitcast_fusion.1
  0.8 0.6 reduce_window_sum.13
  1.5 0.8 reshape.148
  2.4 1.5 copy.51
  4.2 1.1 multiply_convert_fusion.2
  5.3 0.7 convolution_bitcast_fusion.2
  6.0 2.2 copy.58
  8.3 11.6 %all-to-all-start = ((f32[32,128,256]{2,1,0:T(8,128)}), f32[32,128,256]{2,1,0:T(8,128)}, u32[]{:S(2)}, u32[]{:S(2)}) async-start(f32[32,128,256]{2,1,0:T(8,128)} %bitcast.92), calls=%async_computation | async-start | bytes 8388608 | tf_op jit(solution)/shard_map/all_to_all | solution.py:51
  19.9 136.5 %all_gather.7 = f32[32,32,2,32]{3,1,2,0:T(8,128)S(1)} all-gather(f32[1,32,2,32]{3,1,2,0:T(8,128)S(1)} %dynamic_update_slice.4), channel_id=1, replica_groups=mesh['ctx'=32,'head'=8] {'ctx'}, dimensions={0}, use_global_device_ids=true | all-gather | bytes 270336 | tf_op jit(solution)/shard_map/all_gather | solution.py:50
  157.0 0.6 select_reduce_fusion
  157.6 8.4 %fusion = f32[64,64,256]{2,0,1:T(8,128)S(1)} fusion(f32[64,64,256]{2,1,0:T(8,128)} %bitcast.18, pred[64,64]{1,0:T(32,128)(4,1)S(1)} %copy-done.11, pred[64,64]{1,0:T(32,128)(4,1)S(1)} %copy-done.10, f32[64,64]{1,0:T(8,128)S(1)} %select_reduce_fusion), kind=kOutput, calls=%fused_computation | convolution fusion | flops 805314560 | bytes 8413184 | tf_op jit(solution)/shard_map/uv,vpn->upn/dot_general | solution.py:62
  166.0 4.4 %copy.60 = f32[64,64,256]{2,1,0:T(8,128)} copy(f32[64,64,256]{2,0,1:T(8,128)S(1)} %fusion) | data formatting | bytes 8388608 | tf_op jit(solution)/shard_map/uv,vpn->upn/dot_general | solution.py:62
  170.4 7.7 %all-to-all-start.1 = ((f32[32,128,256]{2,1,0:T(8,128)}), f32[32,128,256]{2,1,0:T(8,128)}, u32[]{:S(2)}, u32[]{:S(2)}) async-start(f32[32,128,256]{2,1,0:T(8,128)} %bitcast.94), calls=%async_computation.1 | async-start | bytes 8388608 | tf_op jit(solution)/shard_map/all_to_all | solution.py:77
  178.8 3.6 %fusion.19 = f32[2,128,1,32,64]{1,4,3,0,2:T(8,128)S(1)} fusion(f32[32,2,128]{2,0,1:T(8,128)S(1)} %copy_bitcast_fusion, f32[32,2,128]{2,0,1:T(8,128)S(1)} %reduce_window_sum.13, f32[2,128,128]{2,1,0:T(8,128)S(1)} %fusion.36, pred[128,128]{1,0:T(8,128)(4,1)S(1)} %iota_compare_fusion, bf16[2,128,32,64]{1,0,3,2:T(2,128)(2,1)} %copy-done.2), kind=kOutput, calls=%fused_computation.27 | convolution fusion | flops 139460608 | bytes 3358720 | tf_op jit(solution)/shard_map/gqkts,ksgqp->ktgqp/dot_general | solution.py:94
  182.4 1.2 fusion.35
  183.5 1.3 copy.64
  184.9 1.3 copy.63
  186.4 2.6 copy.62
  189.1 1.3 copy.61
  190.4 73.6 %all-to-all-done.1 = f32[32,128,256]{2,1,0:T(8,128)} async-done(((f32[32,128,256]{2,1,0:T(8,128)}), f32[32,128,256]{2,1,0:T(8,128)}, u32[]{:S(2)}, u32[]{:S(2)}) %all-to-all-start.1) | async-done | bytes 4194336 | tf_op jit(solution)/shard_map/all_to_all | solution.py:77
  264.0 2.6 fusion.12
  266.6 0.5 fusion.8
  267.2 1.8 slice.95
  269.5 1.1 pad_maximum_fusion
  (53 shorter events, 2.5 us)
Async XLA Ops:
  0.0 5.3 %copy-start = (bf16[256,256]{1,0:T(8,128)(2,1)S(1)}, bf16[256,256]{1,0:T(8,128)(2,1)}, u32[]{:S(2)}) copy-start(bf16[256,256]{1,0:T(8,128)(2,1)} %param.13) | copy-start | bytes 393220
  4.2 4.0 %copy-start.2 = (bf16[2,128,32,64]{1,0,3,2:T(2,128)(2,1)}, bf16[2,128,32,64]{1,0,3,2:T(2,128)(2,1)S(1)}, u32[]{:S(2)}) copy-start(bf16[2,128,32,64]{1,0,3,2:T(2,128)(2,1)S(1)} %reshape.145) | copy-start | bytes 3145732
  8.3 148.7 %copy-start.8 = (pred[1,64,64,64]{3,2,1,0:T(32,128)(4,1)S(1)}, pred[1,64,64,64]{3,2,1,0:T(32,128)(4,1)}, u32[]{:S(2)}) copy-start(pred[1,64,64,64]{3,2,1,0:T(32,128)(4,1)} %constant.27.clone) | copy-start | bytes 786436
  8.3 149.3 %copy-start.10 = (pred[64,64]{1,0:T(32,128)(4,1)S(1)}, pred[64,64]{1,0:T(32,128)(4,1)}, u32[]{:S(2)}) copy-start(pred[64,64]{1,0:T(32,128)(4,1)} %constant.32) | copy-start | bytes 12292
  8.3 149.3 %copy-start.11 = (pred[64,64]{1,0:T(32,128)(4,1)S(1)}, pred[64,64]{1,0:T(32,128)(4,1)}, u32[]{:S(2)}) copy-start(pred[64,64]{1,0:T(32,128)(4,1)} %constant.33) | copy-start | bytes 12292
  8.3 149.3 %all-to-all-start = ((f32[32,128,256]{2,1,0:T(8,128)}), f32[32,128,256]{2,1,0:T(8,128)}, u32[]{:S(2)}, u32[]{:S(2)}) async-start(f32[32,128,256]{2,1,0:T(8,128)} %bitcast.92), calls=%async_computation | async-start | bytes 8388608 | tf_op jit(solution)/shard_map/all_to_all | solution.py:51
  170.4 7.7 %copy-start.1 = (bf16[256,2048]{1,0:T(8,128)(2,1)S(1)}, bf16[256,2048]{1,0:T(8,128)(2,1)}, u32[]{:S(2)}) copy-start(bf16[256,2048]{1,0:T(8,128)(2,1)} %param.10) | copy-start | bytes 3145732
  170.4 8.0 %copy-start.13 = (s32[32,1]{0,1:T(1,128)S(1)}, s32[32,1]{0,1:T(1,128)}, u32[]{:S(2)}) copy-start(s32[32,1]{0,1:T(1,128)} %constant.30.clone) | copy-start | bytes 388
  170.4 8.1 %copy-start.9 = (f32[32,256]{1,0:T(8,128)S(1)}, f32[32,256]{1,0:T(8,128)}, u32[]{:S(2)}) copy-start(f32[32,256]{1,0:T(8,128)} %param.12) | copy-start | bytes 98308
  170.4 8.1 %copy-start.7 = (bf16[256,256]{1,0:T(8,128)(2,1)S(1)}, bf16[256,256]{1,0:T(8,128)(2,1)}, u32[]{:S(2)}) copy-start(bf16[256,256]{1,0:T(8,128)(2,1)} %param.14) | copy-start | bytes 393220
  170.4 93.6 %all-to-all-start.1 = ((f32[32,128,256]{2,1,0:T(8,128)}), f32[32,128,256]{2,1,0:T(8,128)}, u32[]{:S(2)}, u32[]{:S(2)}) async-start(f32[32,128,256]{2,1,0:T(8,128)} %bitcast.94), calls=%async_computation.1 | async-start | bytes 8388608 | tf_op jit(solution)/shard_map/all_to_all | solution.py:77
  182.4 3.9 %copy-start.12 = (f32[32]{0:T(128)S(1)}, f32[32]{0:T(128)}, u32[]{:S(2)}) copy-start(f32[32]{0:T(128)} %param.15) | copy-start | bytes 388
  190.4 76.2 %copy-start.3 = (f32[128,2048]{1,0:T(8,128)S(1)}, f32[128,2048]{1,0:T(8,128)}, u32[]{:S(2)}) copy-start(f32[128,2048]{1,0:T(8,128)} %copy.64) | copy-start | bytes 3145732
  264.0 2.6 copy-start.5
  266.6 2.4 copy-start.4
  266.6 2.4 copy-start.6
